TPU v7x, 32 devices: a whole 2x2x4 slice. The times are simulated.
32 devices in a mesh: groups: 2 (over y), rows: 8 (over z, x), heads: 2 (over core).
Axes of the slice: x: 2, y: 2, z: 4, core: 2. Of those that a mesh axis runs over, the one named last changes fastest.
Arguments:
- residual_in: bfloat16 [128, 8192], P(('groups', 'rows'), 'heads'), parts along dimension 0, may hold values from -6 to 6
- query: bfloat16 [128, 8192], P(('groups', 'rows'), 'heads'), parts along dimension 0, may hold values from -120 to 120
- key_cache: bfloat16 [128, 4, 32, 128], P(('groups', 'rows'), 'heads'), parts along dimension 0, may hold values from -4 to 4
- value_cache: bfloat16 [128, 4, 32, 128], P(('groups', 'rows'), 'heads'), parts along dimension 0, may hold values from -5 to 5
- key_new: bfloat16 [128, 4, 128], P(('groups', 'rows'), 'heads'), parts along dimension 0, may hold values from -4 to 4
- value_new: bfloat16 [128, 4, 128], P(('groups', 'rows'), 'heads'), parts along dimension 0, may hold values from -5 to 5
- lengths: int32 [128], P(('groups', 'rows')), parts along dimension 0, may hold values from 2 to 32, as said below
- norm_gain: bfloat16 [8192], replicated, may hold values from 0.3984375 to 1.59375
- hot_gate: bfloat16 [128, 8192], P('heads'), may hold values from -0.0625 to 0.0625
- hot_up: bfloat16 [128, 8192], P('heads'), may hold values from -0.0625 to 0.0625
- hot_down: bfloat16 [128, 8192], P('heads'), may hold values from -0.5 to 0.5
- cold_gate: bfloat16 [512, 8192], P(('rows', 'heads')), may hold values from -0.0625 to 0.0625
- cold_up: bfloat16 [512, 8192], P(('rows', 'heads')), may hold values from -0.0625 to 0.0625
- cold_down: bfloat16 [512, 8192], P(('rows', 'heads')), may hold values from -0.5 to 0.5
- active: int32 [128, 4], P(('groups', 'rows')), parts along dimension 0, may hold values from 0 to 1, as said below
Outputs:
- residual_out: bfloat16 [128, 8192], P(('groups', 'rows'), 'heads'), parts along dimension 0
There are 2 independent parts, one for each index of `groups`. A program takes and returns all parts, laid end to end along the dimension named above; an argument that names none is the same for every part. Nothing has to cross between parts.
Inputs may be any that keep to these rules, and one draw needn't show every extreme that they name: `lengths`: every request has at least two filled slots, and some request has all 32. `active`: 0 or 1; among the 8 requests of one index of rows at most 2 are active on any one cold block, and exactly 2 on some.
All inputs are finite; a program needn't handle non-finite values.
Results may differ from a plain program's by a relative error of at most 0.0085.
Values may be sent and summed in bfloat16 or wider, within the bound.
No kernel may reach another device: no remote copies, remote signals or barrier semaphores. Data moves between devices by JAX's collectives and lax.ppermute only.
A program may use at most 64 MiB of HBM per device.

v0:
```python
import jax
import jax.numpy as jnp
from jax import lax
from jax.sharding import PartitionSpec as P

HD = 128
D = 8192
CAP = 2


def partner(block, axis, bit):
    count = lax.axis_size(axis)
    route = []
    for low in range(count):
        high = low | 1 << bit
        if high != low and high < count:
            route += [(low, high), (high, low)]
    return lax.ppermute(block, axis, route)


def join_halves(half, myself):
    other = partner(half, "heads", 0)
    low_first = jnp.concatenate([half, other], axis=1)
    high_first = jnp.concatenate([other, half], axis=1)
    return jnp.where(myself == 0, low_first, high_first)


def attention_rows(query, key_cache, value_cache, key_new, value_new, lengths):
    count = key_cache.shape[0]
    kv_local = key_cache.shape[1]
    scale_factor = 1.0 / HD**0.5
    queries = query.reshape(count, kv_local, -1, HD)
    scores = (
        jnp.einsum("rgjd,rgpd->rgjp", queries, key_cache, preferred_element_type=jnp.float32)
        * scale_factor
    )
    own_score = (
        jnp.einsum("rgjd,rgd->rgj", queries, key_new, preferred_element_type=jnp.float32)
        * scale_factor
    )
    visible = (jnp.arange(key_cache.shape[2], dtype=jnp.int32)[None, :] < lengths[:, None])[
        :, None, None, :
    ]
    scores = jnp.where(visible, scores, -1e30)
    highest = jnp.maximum(jnp.max(scores, axis=-1), own_score)
    expons = jnp.where(visible, jnp.exp(scores - highest[..., None]), 0.0)
    own_expon = jnp.exp(own_score - highest)
    totals = jnp.sum(expons, axis=-1) + own_expon
    weights = (expons / totals[..., None]).astype(jnp.bfloat16)
    own_weight = (own_expon / totals).astype(jnp.bfloat16)
    blended = jnp.einsum(
        "rgjp,rgpd->rgjd", weights, value_cache, preferred_element_type=jnp.float32
    )
    blended = (
        blended
        + own_weight.astype(jnp.float32)[..., None] * value_new.astype(jnp.float32)[:, :, None, :]
    )
    return blended.reshape(count, -1)


def swiglu_rows(normed, gate_rows, up_rows, down_rows):
    gate = jnp.einsum("rd,nd->rn", normed, gate_rows, preferred_element_type=jnp.float32)
    upper = jnp.einsum("rd,nd->rn", normed, up_rows, preferred_element_type=jnp.float32)
    hidden = (jax.nn.silu(gate) * upper).astype(jnp.bfloat16)
    return jnp.dot(hidden, down_rows, preferred_element_type=jnp.float32)


def collect_rows(selector, returned):
    return lax.dot_general(
        selector,
        returned,
        (((0,), (0,)), ((), ())),
        precision=lax.Precision.HIGHEST,
        preferred_element_type=jnp.float32,
    )


def local(
    residual_in,
    query,
    key_cache,
    value_cache,
    key_new,
    value_new,
    lengths,
    norm_gain,
    hot_gate,
    hot_up,
    hot_down,
    cold_gate,
    cold_up,
    cold_down,
    active,
):
    attended = attention_rows(query, key_cache, value_cache, key_new, value_new, lengths)
    stream = (residual_in.astype(jnp.float32) + attended).astype(jnp.bfloat16)
    half_width = stream.shape[1]
    myself = lax.axis_index("heads")
    local_wide = stream.astype(jnp.float32)
    square_part = jnp.sum(local_wide * local_wide, axis=-1)
    square_total = square_part + partner(square_part, "heads", 0)
    gain_half = lax.dynamic_slice_in_dim(norm_gain, myself * half_width, half_width)
    scaled = (
        local_wide * lax.rsqrt(square_total / D + 1e-05)[:, None] * gain_half.astype(jnp.float32)
    )
    normed = join_halves(scaled.astype(jnp.bfloat16), myself)
    hot_part = swiglu_rows(normed, hot_gate, hot_up, hot_down)
    owner_count = lax.axis_size("rows")
    block_count = active.shape[1]
    request_count = active.shape[0]
    by_block = jnp.transpose(active)
    earlier = jnp.cumsum(by_block, axis=1) - by_block
    slot_ids = jnp.arange(CAP, dtype=jnp.int32)[None, :, None]
    slot_table = by_block[:, None, :] * (earlier[:, None, :] == slot_ids).astype(jnp.int32)
    selector = jnp.repeat(slot_table, owner_count // block_count, axis=0).reshape(
        owner_count * CAP, request_count
    )
    outgoing = jnp.dot(
        selector.astype(jnp.bfloat16), normed, preferred_element_type=jnp.float32
    ).astype(jnp.bfloat16)
    incoming = lax.all_to_all(outgoing, "rows", split_axis=0, concat_axis=0, tiled=True)
    cold_part = swiglu_rows(incoming, cold_gate, cold_up, cold_down)
    selector_wide = selector.astype(jnp.float32)
    kept = lax.dynamic_slice_in_dim(cold_part, myself * half_width, half_width, 1)
    given = lax.dynamic_slice_in_dim(cold_part, (1 - myself) * half_width, half_width, 1)
    owner_sum = kept + partner(given, "heads", 0)
    returned = lax.all_to_all(owner_sum, "rows", split_axis=0, concat_axis=0, tiled=True)
    cold_sum = collect_rows(selector_wide, returned)
    hot_kept = lax.dynamic_slice_in_dim(hot_part, myself * half_width, half_width, 1)
    hot_given = lax.dynamic_slice_in_dim(hot_part, (1 - myself) * half_width, half_width, 1)
    hot_total = hot_kept + partner(hot_given, "heads", 0)
    result = stream.astype(jnp.float32) + hot_total + cold_sum
    return result.astype(jnp.bfloat16)


def solution(mesh):
    return jax.shard_map(
        local,
        mesh=mesh,
        in_specs=(
            P(("groups", "rows"), "heads"),
            P(("groups", "rows"), "heads"),
            P(("groups", "rows"), "heads", None, None),
            P(("groups", "rows"), "heads", None, None),
            P(("groups", "rows"), "heads", None),
            P(("groups", "rows"), "heads", None),
            P(("groups", "rows")),
            P(),
            P("heads", None),
            P("heads", None),
            P("heads", None),
            P(("rows", "heads"), None),
            P(("rows", "heads"), None),
            P(("rows", "heads"), None),
            P(("groups", "rows"), None),
        ),
        out_specs=P(("groups", "rows"), "heads"),
        check_vma=False,
    )
```

profile of v0, /device:TPU:0, one launch (start us, length us, event | category | flops | bytes accessed | tf_op | source)
XLA Modules:
  0.0 45.1 jit_solution(7972570449464875627)
XLA Ops:
  0.0 0.0 copy-start
  0.0 0.0 copy-start.4
  0.0 0.8 %iota_compare_fusion = pred[8,32]{1,0:T(8,128)(4,1)S(1)} fusion(s32[8]{0:T(128)} %param.21), kind=kLoop, calls=%fused_computation.44 | loop fusion | flops 256 | bytes 288 | tf_op jit(solution)/shard_map/lt | solution.py:41
  0.8 1.0 %fusion.14 = f32[8,2,1,16]{3,2,1,0:T(1,128)S(1)} fusion(bf16[8,2,16,128]{3,0,2,1:T(8,128)(2,1)} %bitcast.29, bf16[8,2,128,1]{2,1,0,3:T(2,128)(2,1)} %bitcast.37), kind=kOutput, calls=%fused_computation.26 | convolution fusion | flops 65536 | bytes 70656 | tf_op jit(solution)/shard_map/rgjd,rgd->rgj/dot_general | solution.py:38
  1.8 0.0 copy-done.4
  1.8 1.2 %fusion.36 = (f32[8,2,16]{2,1,0:T(2,128)S(1)}, f32[8,2,16,32]{3,2,1,0:T(8,128)S(1)}) fusion(bf16[8,2,32,128]{3,2,1,0:T(8,128)(2,1)} %param.17, bf16[8,2,16,128]{3,0,2,1:T(8,128)(2,1)S(1)} %bitcast.30, pred[8,32]{1,0:T(8,128)(4,1)S(1)} %iota_compare_fusion), kind=kOutput, calls=%fused_computation.58 | convolution fusion | flops 2121472 | bytes 230656 | tf_op jit(solution)/shard_map/rgjd,rgpd->rgjp/dot_general | solution.py:34
  3.0 0.0 copy-start.9
  3.0 0.2 fusion.9
  3.3 0.0 copy-start.8
  3.3 0.7 %copy-done.8 = bf16[8,2,128]{2,1,0:T(2,128)(2,1)S(1)} copy-done((bf16[8,2,128]{2,1,0:T(2,128)(2,1)S(1)}, bf16[8,2,128]{2,1,0:T(2,128)(2,1)}, u32[]{:S(2)}) %copy-start.8) | copy-done | bytes 4120
  4.0 0.0 copy-done.9
  4.0 0.0 copy-start.5
  4.0 0.0 copy-start.6
  4.0 0.3 convolution_add_fusion
  4.2 0.0 copy-start.7
  4.2 0.5 %copy-done.5 = bf16[8,4096]{1,0:T(8,128)(2,1)S(1)} copy-done((bf16[8,4096]{1,0:T(8,128)(2,1)S(1)}, bf16[8,4096]{1,0:T(8,128)(2,1)}, u32[]{:S(2)}) %copy-start.5) | copy-done | bytes 65560
  4.8 0.2 fusion.3
  5.0 0.5 %collective-permute-start = (f32[8]{0:T(128)S(1)}, f32[8]{0:T(128)S(1)}, u32[]{:S(2)}, u32[]{:S(2)}) collective-permute-start(f32[8]{0:T(128)S(1)} %get-tuple-element.5), channel_id=1, source_target_pairs={{0,1},{1,0},{2,3},{3,2},{4,5},{5,4},{6,7},{7,6},{8,9},{9,8},{10,11... | collective-permute-start | bytes 104 | tf_op jit(solution)/shard_map/ppermute | solution.py:18
  5.5 0.0 copy-done.6
  5.5 0.2 reduce_window_sum.11
  5.7 0.0 copy-done.7
  5.7 0.6 %collective-permute-done = f32[8]{0:T(128)S(1)} collective-permute-done((f32[8]{0:T(128)S(1)}, f32[8]{0:T(128)S(1)}, u32[]{:S(2)}, u32[]{:S(2)}) %collective-permute-start) | collective-permute-done | bytes 64 | tf_op jit(solution)/shard_map/ppermute | solution.py:18
  6.3 0.1 fusion.5
  6.4 0.4 collective-permute-start.1
  6.8 0.9 %collective-permute-done.1 = bf16[8,4096]{1,0:T(8,128)(2,1)S(1)} collective-permute-done((bf16[8,4096]{1,0:T(8,128)(2,1)S(1)}, bf16[8,4096]{1,0:T(8,128)(2,1)S(1)}, u32[]{:S(2)}, u32[]{:S(2)}) %collective-permute-start.1) | collective-permute-done | bytes 65568 | tf_op jit(solution)/shard_map/ppermute | solution.py:18
  7.7 0.2 convolution_convert_fusion
  8.0 0.9 %all_to_all.16 = bf16[8,2,8192]{2,1,0:T(2,128)(2,1)} reshape(bf16[16,8192]{1,0:T(8,128)(2,1)S(1)} %convolution_convert_fusion) | data formatting | bytes 524288 | tf_op jit(solution)/shard_map/all_to_all | solution.py:121
  8.9 7.1 %all-to-all-start = ((bf16[8,2,8192]{2,1,0:T(2,128)(2,1)}), bf16[8,2,8192]{2,1,0:T(2,128)(2,1)S(1)}, u32[]{:S(2)}, u32[]{:S(2)}) async-start(bf16[8,2,8192]{2,1,0:T(2,128)(2,1)} %all_to_all.16), calls=%async_computation | async-start | bytes 524288 | tf_op jit(solution)/shard_map/all_to_all | solution.py:121
  16.0 0.0 copy-done.1
  16.0 0.4 fusion.33
  16.3 8.9 %all-to-all-done = bf16[8,2,8192]{2,1,0:T(2,128)(2,1)S(1)} async-done(((bf16[8,2,8192]{2,1,0:T(2,128)(2,1)}), bf16[8,2,8192]{2,1,0:T(2,128)(2,1)S(1)}, u32[]{:S(2)}, u32[]{:S(2)}) %all-to-all-start) | async-done | bytes 262176 | tf_op jit(solution)/shard_map/all_to_all | solution.py:121
  25.3 0.1 all_to_all.18
  25.4 0.0 copy-done.3
  25.4 0.2 fusion.37
  25.6 1.9 %fusion.2 = f32[16,8192]{1,0:T(8,128)S(1)} fusion(bf16[32,8192]{1,0:T(8,128)(2,1)} %param.28, bf16[16,8192]{1,0:T(8,128)(2,1)S(1)} %all_to_all.18, bf16[32,8192]{1,0:T(8,128)(2,1)} %param.27, f32[16,32]{1,0:T(8,128)S(1)} %fusion.37), kind=kOutput, calls=%fused_computation.6 | convolution fusion | flops 16780288 | bytes 1837056 | tf_op jit(solution)/shard_map/dot_general | solution.py:65
  27.5 0.1 collective-permute-start.3
  27.6 0.0 copy-done
  27.6 0.0 copy-done.2
  27.6 0.9 %fusion.27 = f32[8,8192]{1,0:T(8,128)S(1)} fusion(bf16[64,8192]{1,0:T(8,128)(2,1)S(1)} %copy-done, f32[8,64]{1,0:T(8,128)S(1)} %fusion.33, bf16[64,8192]{1,0:T(8,128)(2,1)S(1)} %copy-done.2, bf16[8,4096]{1,0:T(8,128)(2,1)S(1)} %collective-permute-done.1, bf16[8,4096]{1,0:T(8,128)(2,1)S(1)} %fusion.5, pred[]{:T(512)S(6)} %eq.16), kind=kOutput, calls=%fused_computation.46 | convolution fusion | flops 17370112 | bytes 2492417 | tf_op jit(solution)/shard_map/dot_general | solution.py:65
  28.5 0.7 %collective-permute-done.3 = f32[16,4096]{1,0:T(8,128)} collective-permute-done((f32[16,4096]{1,0:T(8,128)S(1)}, f32[16,4096]{1,0:T(8,128)}, u32[]{:S(2)}, u32[]{:S(2)}) %collective-permute-start.3) | collective-permute-done | bytes 262176 | tf_op jit(solution)/shard_map/ppermute | solution.py:18
  29.3 1.0 %dynamic-slice_add_fusion = f32[16,4096]{1,0:T(8,128)S(1)} fusion(f32[16,4096]{1,0:T(8,128)} %collective-permute-done.3, f32[16,8192]{1,0:T(8,128)S(1)} %fusion.2, s32[]{:T(128)S(6)} %select_n.27), kind=kLoop, calls=%fused_computation.7 | loop fusion | flops 65536 | bytes 786436 | tf_op jit(solution)/shard_map/add | solution.py:126
  30.2 0.9 %all_to_all.19 = f32[8,2,4096]{2,1,0:T(2,128)} reshape(f32[16,4096]{1,0:T(8,128)S(1)} %dynamic-slice_add_fusion) | data formatting | bytes 524288 | tf_op jit(solution)/shard_map/all_to_all | solution.py:127
  31.1 3.6 %all-to-all-start.1 = ((f32[8,2,4096]{2,1,0:T(2,128)}), f32[8,2,4096]{2,1,0:T(2,128)S(1)}, u32[]{:S(2)}, u32[]{:S(2)}) async-start(f32[8,2,4096]{2,1,0:T(2,128)} %all_to_all.19), calls=%async_computation.1 | async-start | bytes 524288 | tf_op jit(solution)/shard_map/all_to_all | solution.py:127
  34.7 0.1 collective-permute-start.2
  34.8 9.2 %all-to-all-done.1 = f32[8,2,4096]{2,1,0:T(2,128)S(1)} async-done(((f32[8,2,4096]{2,1,0:T(2,128)}), f32[8,2,4096]{2,1,0:T(2,128)S(1)}, u32[]{:S(2)}, u32[]{:S(2)}) %all-to-all-start.1) | async-done | bytes 262176 | tf_op jit(solution)/shard_map/all_to_all | solution.py:127
  44.0 0.2 all_to_all.21
  44.1 0.0 collective-permute-done.2
  44.2 1.0 %fusion.7 = bf16[8,4096]{1,0:T(8,128)(2,1)} fusion(bf16[8,4096]{1,0:T(8,128)(2,1)S(1)} %get-tuple-element.6, f32[8,4096]{1,0:T(8,128)S(1)} %collective-permute-done.2, f32[8,8192]{1,0:T(8,128)S(1)} %fusion.27, s32[]{:T(128)S(6)} %select_n.27, f32[16,8]{1,0:T(8,128)S(1)} %bitcast.31, f32[16,4096]{1,0:T(8,128)S(1)} %all_to_all.21), kind=kOutput, calls=%fused_computation.15 | convolution fusion | flops 6455296 | bytes 655876 | tf_op jit(solution)/shard_map/dot_general | solution.py:69
  (14 shorter events, 0.1 us)
Async XLA Ops:
  0.0 27.6 %copy-start = (bf16[64,8192]{1,0:T(8,128)(2,1)S(1)}, bf16[64,8192]{1,0:T(8,128)(2,1)}, u32[]{:S(2)}) copy-start(bf16[64,8192]{1,0:T(8,128)(2,1)} %param.25) | copy-start | bytes 3145732
  0.0 1.8 %copy-start.4 = (bf16[8,4096]{1,0:T(8,128)(2,1)S(1)}, bf16[8,4096]{1,0:T(8,128)(2,1)}, u32[]{:S(2)}) copy-start(bf16[8,4096]{1,0:T(8,128)(2,1)} %param.16) | copy-start | bytes 196612
  3.0 1.0 %copy-start.9 = (bf16[8,2,32,128]{3,2,1,0:T(8,128)(2,1)S(1)}, bf16[8,2,32,128]{3,2,1,0:T(8,128)(2,1)}, u32[]{:S(2)}) copy-start(bf16[8,2,32,128]{3,2,1,0:T(8,128)(2,1)} %param.18) | copy-start | bytes 393220
  3.3 0.7 %copy-start.8 = (bf16[8,2,128]{2,1,0:T(2,128)(2,1)S(1)}, bf16[8,2,128]{2,1,0:T(2,128)(2,1)}, u32[]{:S(2)}) copy-start(bf16[8,2,128]{2,1,0:T(2,128)(2,1)} %param.20) | copy-start | bytes 12292
  4.0 0.8 %copy-start.5 = (bf16[8,4096]{1,0:T(8,128)(2,1)S(1)}, bf16[8,4096]{1,0:T(8,128)(2,1)}, u32[]{:S(2)}) copy-start(bf16[8,4096]{1,0:T(8,128)(2,1)} %param.15) | copy-start | bytes 196612
  4.0 1.5 %copy-start.6 = (s32[8,4]{0,1:T(4,128)S(1)}, s32[8,4]{0,1:T(4,128)}, u32[]{:S(2)}) copy-start(s32[8,4]{0,1:T(4,128)} %param.29) | copy-start | bytes 388
  4.2 1.5 %copy-start.7 = (bf16[8192]{0:T(1024)(128)(2,1)S(1)}, bf16[8192]{0:T(1024)(128)(2,1)}, u32[]{:S(2)}) copy-start(bf16[8192]{0:T(1024)(128)(2,1)} %param.22) | copy-start | bytes 49156
  4.8 11.2 %copy-start.1 = (bf16[64,8192]{1,0:T(8,128)(2,1)S(1)}, bf16[64,8192]{1,0:T(8,128)(2,1)}, u32[]{:S(2)}) copy-start(bf16[64,8192]{1,0:T(8,128)(2,1)} %param.24) | copy-start | bytes 3145732
  5.0 1.3 %collective-permute-start = (f32[8]{0:T(128)S(1)}, f32[8]{0:T(128)S(1)}, u32[]{:S(2)}, u32[]{:S(2)}) collective-permute-start(f32[8]{0:T(128)S(1)} %get-tuple-element.5), channel_id=1, source_target_pairs={{0,1},{1,0},{2,3},{3,2},{4,5},{5,4},{6,7},{7,6},{8,9},{9,8},{10,11... | collective-permute-start | bytes 104 | tf_op jit(solution)/shard_map/ppermute | solution.py:18
  6.4 1.3 %collective-permute-start.1 = (bf16[8,4096]{1,0:T(8,128)(2,1)S(1)}, bf16[8,4096]{1,0:T(8,128)(2,1)S(1)}, u32[]{:S(2)}, u32[]{:S(2)}) collective-permute-start(bf16[8,4096]{1,0:T(8,128)(2,1)S(1)} %fusion.5), channel_id=1, source_target_pairs={{0,1},{1,0},{2,3},{3,2},{4,5},{5,4},{6,7},{7,6},{8,9},{9,8},{10,11... | collective-permute-start | bytes 196616 | tf_op jit(solution)/shard_map/ppermute | solution.py:18
  8.9 16.4 %all-to-all-start = ((bf16[8,2,8192]{2,1,0:T(2,128)(2,1)}), bf16[8,2,8192]{2,1,0:T(2,128)(2,1)S(1)}, u32[]{:S(2)}, u32[]{:S(2)}) async-start(bf16[8,2,8192]{2,1,0:T(2,128)(2,1)} %all_to_all.16), calls=%async_computation | async-start | bytes 524288 | tf_op jit(solution)/shard_map/all_to_all | solution.py:121
  16.3 9.0 %copy-start.3 = (bf16[32,8192]{1,0:T(8,128)(2,1)S(1)}, bf16[32,8192]{1,0:T(8,128)(2,1)}, u32[]{:S(2)}) copy-start(bf16[32,8192]{1,0:T(8,128)(2,1)} %param.26) | copy-start | bytes 1572868
  25.6 2.0 %copy-start.2 = (bf16[64,8192]{1,0:T(8,128)(2,1)S(1)}, bf16[64,8192]{1,0:T(8,128)(2,1)}, u32[]{:S(2)}) copy-start(bf16[64,8192]{1,0:T(8,128)(2,1)} %param.23) | copy-start | bytes 3145732
  27.5 1.7 %collective-permute-start.3 = (f32[16,4096]{1,0:T(8,128)S(1)}, f32[16,4096]{1,0:T(8,128)}, u32[]{:S(2)}, u32[]{:S(2)}) collective-permute-start(f32[16,4096]{1,0:T(8,128)S(1)} %constant_dynamic-slice_fusion), channel_id=1, source_target_pairs={{0,1},{1,0},{2,3},{3,2},{4,5},{5,4},{6,7},{7,6},{8,9},{9,8},{10,11... | collective-permute-start | bytes 786440 | tf_op jit(solution)/shard_map/ppermute | solution.py:18
  31.1 12.9 %all-to-all-start.1 = ((f32[8,2,4096]{2,1,0:T(2,128)}), f32[8,2,4096]{2,1,0:T(2,128)S(1)}, u32[]{:S(2)}, u32[]{:S(2)}) async-start(f32[8,2,4096]{2,1,0:T(2,128)} %all_to_all.19), calls=%async_computation.1 | async-start | bytes 524288 | tf_op jit(solution)/shard_map/all_to_all | solution.py:127
  34.7 9.4 %collective-permute-start.2 = (f32[8,4096]{1,0:T(8,128)S(1)}, f32[8,4096]{1,0:T(8,128)S(1)}, u32[]{:S(2)}, u32[]{:S(2)}) collective-permute-start(f32[8,4096]{1,0:T(8,128)S(1)} %constant_dynamic-slice_fusion.1), channel_id=1, source_target_pairs={{0,1},{1,0},{2,3},{3,2},{4,5},{5,4},{6,7},{7,6},{8,9},{9,8},{10,11... | collective-permute-start | bytes 393224 | tf_op jit(solution)/shard_map/ppermute | solution.py:18
where the time goes:
time: 45.6 us; the launch traced here: 45.1 us
  waiting for transfers between devices  20.4 us (45%)
  starting transfers between devices  11.7 us (26%)
  matrix products  6.98 us (15%)
  local copies, waits for them, and re-layouts  3.33 us (7%)
  other arithmetic  2.53 us (6%)
    all_to_all x1, waiting for transfers between devices, local(): lax.all_to_all(owner_sum, 'rows', split_axis=0, concat_axis=0, tiled=True)  9.17 us
    all_to_all x1, waiting for transfers between devices, local(): lax.all_to_all(outgoing, 'rows', split_axis=0, concat_axis=0, tiled=True)  8.91 us
    all_to_all x1, starting transfers between devices, local(): lax.all_to_all(outgoing, 'rows', split_axis=0, concat_axis=0, tiled=True)  7.1 us
    all_to_all x1, starting transfers between devices, local(): lax.all_to_all(owner_sum, 'rows', split_axis=0, concat_axis=0, tiled=True)  3.59 us
    dot_general x2, matrix products, swiglu_rows(): return jnp.dot(hidden, down_rows, preferred_element_type=jnp.float32)  2.78 us
    ppermute x4, waiting for transfers between devices, partner(): return lax.ppermute(block, axis, route)  2.3 us
    unnamed x20, local copies, waits for them, and re-layouts  1.24 us
    dot_general x1, matrix products, attention_rows(): jnp.einsum('rgjd,rgpd->rgjp', queries, key_cache, preferred_element_type=...  1.17 us
  transfers between devices with their start and end apart: 6, of which 5 were waited for; matrix products, arithmetic and copies ran while one was open for 3% of the time, Pallas kernels for 0%

commit v1 on v0

--- a/solution.py
+++ b/solution.py
@@ -6,6 +6,28 @@
 HD = 128
 D = 8192
 CAP = 2
+
+
+def split_up(value, dim, size):
+    before, after = (value.shape[:dim], value.shape[dim + 1 :])
+    return jnp.moveaxis(value.reshape(*before, size, -1, *after), dim, 0)
+
+
+def in_order(blocks, dim):
+    lengths = list(blocks.shape[1:])
+    lengths[dim] *= blocks.shape[0]
+    return jnp.moveaxis(blocks, 0, dim).reshape(lengths)
+
+
+def exchange_in_pairs(x, axis, split_dim, concat_dim):
+    size, place = (lax.axis_size(axis), lax.axis_index(axis))
+    blocks = split_up(x, split_dim, size)
+    outs = [blocks[place]]
+    for turn in range(1, size):
+        sent = blocks[place ^ turn]
+        outs.append(lax.ppermute(sent, axis, [(i, i ^ turn) for i in range(size)]))
+    blocks = jnp.stack(outs)[place ^ jnp.arange(size)]
+    return in_order(blocks, concat_dim)
 
 
 def partner(block, axis, bit):
@@ -124,7 +146,7 @@
     kept = lax.dynamic_slice_in_dim(cold_part, myself * half_width, half_width, 1)
     given = lax.dynamic_slice_in_dim(cold_part, (1 - myself) * half_width, half_width, 1)
     owner_sum = kept + partner(given, "heads", 0)
-    returned = lax.all_to_all(owner_sum, "rows", split_axis=0, concat_axis=0, tiled=True)
+    returned = exchange_in_pairs(owner_sum, "rows", 0, 0)
     cold_sum = collect_rows(selector_wide, returned)
     hot_kept = lax.dynamic_slice_in_dim(hot_part, myself * half_width, half_width, 1)
     hot_given = lax.dynamic_slice_in_dim(hot_part, (1 - myself) * half_width, half_width, 1)

time: 45.6 us -> 48.6 us (1.066)
  starting transfers between devices: 11.7 us -> 19.5 us
  waiting for transfers between devices: 20.4 us -> 15.3 us
    ppermute x0 -> x7, starting transfers between devices: none -> 11.4 us  [exchange_in_pairs(): outs.append(lax.ppermute(sent, axis, [(i, i ^ turn) for i in range(size)]))]
    all_to_all x1 -> x0, waiting for transfers between devices: 9.17 us -> none  [local(): lax.all_to_all(owner_sum, 'rows', split_axis=0, concat_axis=0, tiled=True)]
    ppermute x0 -> x7, waiting for transfers between devices: none -> 4.15 us  [exchange_in_pairs(): outs.append(lax.ppermute(sent, axis, [(i, i ^ turn) for i in range(size)]))]
    all_to_all x1 -> x0, starting transfers between devices: 3.59 us -> none  [local(): lax.all_to_all(owner_sum, 'rows', split_axis=0, concat_axis=0, tiled=True)]
    all_to_all x2 -> x0, local copies, waits for them, and re-layouts: 1.04 us -> none  [local(): lax.all_to_all(owner_sum, 'rows', split_axis=0, concat_axis=0, tiled=True)]
    gather x0 -> x1, local copies, waits for them, and re-layouts: none -> 0.83 us  [exchange_in_pairs(): blocks = jnp.stack(outs)[place ^ jnp.arange(size)]]
    unnamed x20 -> x26, local copies, waits for them, and re-layouts: 1.24 us -> 1.3 us
  transfers between devices with their start and end apart: 6 -> 12, of which waited for: 5 -> 6; matrix products, arithmetic and copies ran while one was open for 3% -> 5% of each run, Pallas kernels for 0% -> 0%
where the time goes in v1:
time: 48.6 us; the launch traced here: 48.2 us
  starting transfers between devices  19.5 us (40%)
  waiting for transfers between devices  15.3 us (31%)
  matrix products  6.98 us (14%)
  local copies, waits for them, and re-layouts  3.54 us (7%)
  other arithmetic  2.55 us (5%)
    ppermute x7, starting transfers between devices, exchange_in_pairs(): outs.append(lax.ppermute(sent, axis, [(i, i ^ turn) for i in range(size)]))  11.4 us
    all_to_all x1, waiting for transfers between devices, local(): lax.all_to_all(outgoing, 'rows', split_axis=0, concat_axis=0, tiled=True)  8.89 us
    all_to_all x1, starting transfers between devices, local(): lax.all_to_all(outgoing, 'rows', split_axis=0, concat_axis=0, tiled=True)  7.1 us
    ppermute x7, waiting for transfers between devices, exchange_in_pairs(): outs.append(lax.ppermute(sent, axis, [(i, i ^ turn) for i in range(size)]))  4.15 us
    dot_general x2, matrix products, swiglu_rows(): return jnp.dot(hidden, down_rows, preferred_element_type=jnp.float32)  2.78 us
    ppermute x4, waiting for transfers between devices, partner(): return lax.ppermute(block, axis, route)  2.3 us
    unnamed x26, local copies, waits for them, and re-layouts  1.3 us
    dot_general x1, matrix products, attention_rows(): jnp.einsum('rgjd,rgpd->rgjp', queries, key_cache, preferred_element_type=...  1.17 us
  transfers between devices with their start and end apart: 12, of which 6 were waited for; matrix products, arithmetic and copies ran while one was open for 5% of the time, Pallas kernels for 0%

profile of v1, /device:TPU:0, one launch (start us, length us, event | category | flops | bytes accessed | tf_op | source)
XLA Modules:
  0.0 48.2 jit_solution(908897301201448206)
XLA Ops:
  0.0 0.8 %iota_compare_fusion = pred[8,32]{1,0:T(8,128)(4,1)S(1)} fusion(s32[8]{0:T(128)} %param.21), kind=kLoop, calls=%fused_computation.61 | loop fusion | flops 256 | bytes 288 | tf_op jit(solution)/shard_map/lt | solution.py:63
  0.8 1.0 %fusion.14 = f32[8,2,1,16]{3,2,1,0:T(1,128)S(1)} fusion(bf16[8,2,16,128]{3,0,2,1:T(8,128)(2,1)} %bitcast.59, bf16[8,2,128,1]{2,1,0,3:T(2,128)(2,1)} %bitcast.67), kind=kOutput, calls=%fused_computation.27 | convolution fusion | flops 65536 | bytes 70656 | tf_op jit(solution)/shard_map/rgjd,rgd->rgj/dot_general | solution.py:60
  1.8 1.2 %fusion.37 = (f32[8,2,16]{2,1,0:T(2,128)S(1)}, f32[8,2,16,32]{3,2,1,0:T(8,128)S(1)}) fusion(bf16[8,2,32,128]{3,2,1,0:T(8,128)(2,1)} %param.17, bf16[8,2,16,128]{3,0,2,1:T(8,128)(2,1)S(1)} %bitcast.60, pred[8,32]{1,0:T(8,128)(4,1)S(1)} %iota_compare_fusion), kind=kOutput, calls=%fused_computation.77 | convolution fusion | flops 2121472 | bytes 230656 | tf_op jit(solution)/shard_map/rgjd,rgpd->rgjp/dot_general | solution.py:56
  3.0 0.0 copy-start.9
  3.0 0.2 fusion.9
  3.3 0.0 copy-start.8
  3.3 0.7 %copy-done.8 = bf16[8,2,128]{2,1,0:T(2,128)(2,1)S(1)} copy-done((bf16[8,2,128]{2,1,0:T(2,128)(2,1)S(1)}, bf16[8,2,128]{2,1,0:T(2,128)(2,1)}, u32[]{:S(2)}) %copy-start.8) | copy-done | bytes 4120
  4.0 0.0 copy-start.6
  4.0 0.3 convolution_add_fusion
  4.2 0.0 copy-start.7
  4.2 0.5 %copy-done.5 = bf16[8,4096]{1,0:T(8,128)(2,1)S(1)} copy-done((bf16[8,4096]{1,0:T(8,128)(2,1)S(1)}, bf16[8,4096]{1,0:T(8,128)(2,1)}, u32[]{:S(2)}) %copy-start.5) | copy-done | bytes 65560
  4.8 0.2 fusion.3
  5.0 0.5 %collective-permute-start = (f32[8]{0:T(128)S(1)}, f32[8]{0:T(128)S(1)}, u32[]{:S(2)}, u32[]{:S(2)}) collective-permute-start(f32[8]{0:T(128)S(1)} %get-tuple-element.5), channel_id=1, source_target_pairs={{0,1},{1,0},{2,3},{3,2},{4,5},{5,4},{6,7},{7,6},{8,9},{9,8},{10,11... | collective-permute-start | bytes 104 | tf_op jit(solution)/shard_map/ppermute | solution.py:40
  5.5 0.2 reduce_window_sum.11
  5.7 0.6 %collective-permute-done = f32[8]{0:T(128)S(1)} collective-permute-done((f32[8]{0:T(128)S(1)}, f32[8]{0:T(128)S(1)}, u32[]{:S(2)}, u32[]{:S(2)}) %collective-permute-start) | collective-permute-done | bytes 64 | tf_op jit(solution)/shard_map/ppermute | solution.py:40
  6.3 0.1 fusion.5
  6.4 0.4 collective-permute-start.1
  6.8 0.9 %collective-permute-done.1 = bf16[8,4096]{1,0:T(8,128)(2,1)S(1)} collective-permute-done((bf16[8,4096]{1,0:T(8,128)(2,1)S(1)}, bf16[8,4096]{1,0:T(8,128)(2,1)S(1)}, u32[]{:S(2)}, u32[]{:S(2)}) %collective-permute-start.1) | collective-permute-done | bytes 65568 | tf_op jit(solution)/shard_map/ppermute | solution.py:40
  7.7 0.2 convolution_convert_fusion
  8.0 0.9 %all_to_all.8 = bf16[8,2,8192]{2,1,0:T(2,128)(2,1)} reshape(bf16[16,8192]{1,0:T(8,128)(2,1)S(1)} %convolution_convert_fusion) | data formatting | bytes 524288 | tf_op jit(solution)/shard_map/all_to_all | solution.py:143
  8.8 7.1 %all-to-all-start = ((bf16[8,2,8192]{2,1,0:T(2,128)(2,1)}), bf16[8,2,8192]{2,1,0:T(2,128)(2,1)S(1)}, u32[]{:S(2)}, u32[]{:S(2)}) async-start(bf16[8,2,8192]{2,1,0:T(2,128)(2,1)} %all_to_all.8), calls=%async_computation | async-start | bytes 524288 | tf_op jit(solution)/shard_map/all_to_all | solution.py:143
  16.0 0.4 fusion.34
  16.4 8.9 %all-to-all-done = bf16[8,2,8192]{2,1,0:T(2,128)(2,1)S(1)} async-done(((bf16[8,2,8192]{2,1,0:T(2,128)(2,1)}), bf16[8,2,8192]{2,1,0:T(2,128)(2,1)S(1)}, u32[]{:S(2)}, u32[]{:S(2)}) %all-to-all-start) | async-done | bytes 262176 | tf_op jit(solution)/shard_map/all_to_all | solution.py:143
  25.2 0.1 all_to_all.10
  25.4 0.2 fusion.38
  25.6 1.9 %fusion.2 = f32[16,8192]{1,0:T(8,128)S(1)} fusion(bf16[32,8192]{1,0:T(8,128)(2,1)} %param.28, bf16[16,8192]{1,0:T(8,128)(2,1)S(1)} %all_to_all.10, bf16[32,8192]{1,0:T(8,128)(2,1)} %param.27, f32[16,32]{1,0:T(8,128)S(1)} %fusion.38), kind=kOutput, calls=%fused_computation.7 | convolution fusion | flops 16780288 | bytes 1837056 | tf_op jit(solution)/shard_map/dot_general | solution.py:87
  27.5 0.1 collective-permute-start.3
  27.6 0.9 %fusion.27 = f32[8,8192]{1,0:T(8,128)S(1)} fusion(bf16[64,8192]{1,0:T(8,128)(2,1)S(1)} %copy-done, f32[8,64]{1,0:T(8,128)S(1)} %fusion.34, bf16[64,8192]{1,0:T(8,128)(2,1)S(1)} %copy-done.2, bf16[8,4096]{1,0:T(8,128)(2,1)S(1)} %collective-permute-done.1, bf16[8,4096]{1,0:T(8,128)(2,1)S(1)} %fusion.5, pred[]{:T(512)S(6)} %eq.16), kind=kOutput, calls=%fused_computation.66 | convolution fusion | flops 17370112 | bytes 2492417 | tf_op jit(solution)/shard_map/dot_general | solution.py:87
  28.5 0.7 %collective-permute-done.3 = f32[16,4096]{1,0:T(8,128)} collective-permute-done((f32[16,4096]{1,0:T(8,128)S(1)}, f32[16,4096]{1,0:T(8,128)}, u32[]{:S(2)}, u32[]{:S(2)}) %collective-permute-start.3) | collective-permute-done | bytes 262176 | tf_op jit(solution)/shard_map/ppermute | solution.py:40
  29.2 1.0 %dynamic-slice_add_fusion = f32[16,4096]{1,0:T(8,128)S(1)} fusion(f32[16,4096]{1,0:T(8,128)} %collective-permute-done.3, f32[16,8192]{1,0:T(8,128)S(1)} %fusion.2, s32[]{:T(128)S(6)} %select_n.61), kind=kLoop, calls=%fused_computation.8 | loop fusion | flops 65536 | bytes 786436 | tf_op jit(solution)/shard_map/add | solution.py:148
  30.2 0.2 reshape.59
  30.4 1.5 %collective-permute-start.4 = (f32[2,4096]{1,0:T(2,128)S(1)}, f32[2,4096]{1,0:T(2,128)S(1)}, u32[]{:S(2)}, u32[]{:S(2)}) collective-permute-start(f32[2,4096]{1,0:T(2,128)S(1)} %get-tuple-element.13), channel_id=1, source_target_pairs={{0,2},{2,0},{4,6},{6,4},{8,10},{10,8},{12,14},{14,12},{1,3},{3,1},... | collective-permute-start | bytes 98312 | tf_op jit(solution)/shard_map/ppermute | solution.py:28
  31.9 0.1 collective-permute-start.2
  32.0 0.1 collective-permute-start.5
  32.1 2.0 %collective-permute-start.6 = (f32[2,4096]{1,0:T(2,128)S(1)}, f32[2,4096]{1,0:T(2,128)S(1)}, u32[]{:S(2)}, u32[]{:S(2)}) collective-permute-start(f32[2,4096]{1,0:T(2,128)S(1)} %get-tuple-element.11), channel_id=1, source_target_pairs={{0,6},{2,4},{4,2},{6,0},{8,14},{10,12},{12,10},{14,8},{1,7},{3,5},... | collective-permute-start | bytes 98312 | tf_op jit(solution)/shard_map/ppermute | solution.py:28
  34.1 1.0 %collective-permute-start.7 = (f32[2,4096]{1,0:T(2,128)S(1)}, f32[2,4096]{1,0:T(2,128)S(1)}, u32[]{:S(2)}, u32[]{:S(2)}) collective-permute-start(f32[2,4096]{1,0:T(2,128)S(1)} %get-tuple-element.10), channel_id=1, source_target_pairs={{0,8},{2,10},{4,12},{6,14},{8,0},{10,2},{12,4},{14,6},{1,9},{3,11}... | collective-permute-start | bytes 98312 | tf_op jit(solution)/shard_map/ppermute | solution.py:28
  35.2 0.0 collective-permute-done.4
  35.2 2.7 %collective-permute-start.8 = (f32[2,4096]{1,0:T(2,128)S(1)}, f32[2,4096]{1,0:T(2,128)S(1)}, u32[]{:S(2)}, u32[]{:S(2)}) collective-permute-start(f32[2,4096]{1,0:T(2,128)S(1)} %get-tuple-element.9), channel_id=1, source_target_pairs={{0,10},{2,8},{4,14},{6,12},{8,2},{10,0},{12,6},{14,4},{1,11},{3,9}... | collective-permute-start | bytes 98312 | tf_op jit(solution)/shard_map/ppermute | solution.py:28
  37.9 0.0 collective-permute-done.5
  37.9 1.5 %collective-permute-start.9 = (f32[2,4096]{1,0:T(2,128)S(1)}, f32[2,4096]{1,0:T(2,128)S(1)}, u32[]{:S(2)}, u32[]{:S(2)}) collective-permute-start(f32[2,4096]{1,0:T(2,128)S(1)} %get-tuple-element.8), channel_id=1, source_target_pairs={{0,12},{2,14},{4,8},{6,10},{8,4},{10,6},{12,0},{14,2},{1,13},{3,15... | collective-permute-start | bytes 98312 | tf_op jit(solution)/shard_map/ppermute | solution.py:28
  39.5 0.0 collective-permute-done.6
  39.5 2.5 %collective-permute-start.10 = (f32[2,4096]{1,0:T(2,128)S(1)}, f32[2,4096]{1,0:T(2,128)S(1)}, u32[]{:S(2)}, u32[]{:S(2)}) collective-permute-start(f32[2,4096]{1,0:T(2,128)S(1)} %get-tuple-element.7), channel_id=1, source_target_pairs={{0,14},{2,12},{4,10},{6,8},{8,6},{10,4},{12,2},{14,0},{1,15},{3,13... | collective-permute-start | bytes 98312 | tf_op jit(solution)/shard_map/ppermute | solution.py:28
  42.0 0.0 collective-permute-done.7
  42.0 1.7 %collective-permute-done.9 = f32[2,4096]{1,0:T(2,128)S(1)} collective-permute-done((f32[2,4096]{1,0:T(2,128)S(1)}, f32[2,4096]{1,0:T(2,128)S(1)}, u32[]{:S(2)}, u32[]{:S(2)}) %collective-permute-start.9) | collective-permute-done | bytes 32800 | tf_op jit(solution)/shard_map/ppermute | solution.py:28
  43.7 2.4 %collective-permute-done.10 = f32[2,4096]{1,0:T(2,128)S(1)} collective-permute-done((f32[2,4096]{1,0:T(2,128)S(1)}, f32[2,4096]{1,0:T(2,128)S(1)}, u32[]{:S(2)}, u32[]{:S(2)}) %collective-permute-start.10) | collective-permute-done | bytes 32800 | tf_op jit(solution)/shard_map/ppermute | solution.py:28
  46.2 0.8 %gather_fusion = f32[8,2,4096]{2,1,0:T(2,128)S(1)} fusion(f32[8,2,4096]{2,1,0:T(2,128)S(1)} %bitcast_dynamic-update-slice_fusion, s32[1024]{0:T(1024)S(1)} %pad_clamp_fusion), kind=kCustom, calls=%fused_computation | custom fusion | bytes 524320 | tf_op jit(solution)/shard_map/gather | solution.py:29
  47.0 0.2 reshape.60
  47.2 1.0 %fusion.7 = bf16[8,4096]{1,0:T(8,128)(2,1)} fusion(bf16[8,4096]{1,0:T(8,128)(2,1)S(1)} %get-tuple-element.6, f32[8,4096]{1,0:T(8,128)S(1)} %collective-permute-done.2, f32[8,8192]{1,0:T(8,128)S(1)} %fusion.27, s32[]{:T(128)S(6)} %select_n.61, f32[16,8]{1,0:T(8,128)S(1)} %bitcast.61, f32[16,4096]{1,0:T(8,128)S(1)} %reshape.60), kind=kOutput, calls=%fused_computation.16 | convolution fusion | flops 6455296 | bytes 655876 | tf_op jit(solution)/shard_map/dot_general | solution.py:91
  (37 shorter events, 0.3 us)
Async XLA Ops:
  0.0 27.6 %copy-start = (bf16[64,8192]{1,0:T(8,128)(2,1)S(1)}, bf16[64,8192]{1,0:T(8,128)(2,1)}, u32[]{:S(2)}) copy-start(bf16[64,8192]{1,0:T(8,128)(2,1)} %param.25) | copy-start | bytes 3145732
  0.0 1.8 %copy-start.4 = (bf16[8,4096]{1,0:T(8,128)(2,1)S(1)}, bf16[8,4096]{1,0:T(8,128)(2,1)}, u32[]{:S(2)}) copy-start(bf16[8,4096]{1,0:T(8,128)(2,1)} %param.16) | copy-start | bytes 196612
  3.0 1.0 %copy-start.9 = (bf16[8,2,32,128]{3,2,1,0:T(8,128)(2,1)S(1)}, bf16[8,2,32,128]{3,2,1,0:T(8,128)(2,1)}, u32[]{:S(2)}) copy-start(bf16[8,2,32,128]{3,2,1,0:T(8,128)(2,1)} %param.18) | copy-start | bytes 393220
  3.3 0.7 %copy-start.8 = (bf16[8,2,128]{2,1,0:T(2,128)(2,1)S(1)}, bf16[8,2,128]{2,1,0:T(2,128)(2,1)}, u32[]{:S(2)}) copy-start(bf16[8,2,128]{2,1,0:T(2,128)(2,1)} %param.20) | copy-start | bytes 12292
  4.0 0.8 %copy-start.5 = (bf16[8,4096]{1,0:T(8,128)(2,1)S(1)}, bf16[8,4096]{1,0:T(8,128)(2,1)}, u32[]{:S(2)}) copy-start(bf16[8,4096]{1,0:T(8,128)(2,1)} %param.15) | copy-start | bytes 196612
  4.0 1.5 %copy-start.6 = (s32[8,4]{0,1:T(4,128)S(1)}, s32[8,4]{0,1:T(4,128)}, u32[]{:S(2)}) copy-start(s32[8,4]{0,1:T(4,128)} %param.29) | copy-start | bytes 388
  4.2 1.5 %copy-start.7 = (bf16[8192]{0:T(1024)(128)(2,1)S(1)}, bf16[8192]{0:T(1024)(128)(2,1)}, u32[]{:S(2)}) copy-start(bf16[8192]{0:T(1024)(128)(2,1)} %param.22) | copy-start | bytes 49156
  4.8 11.2 %copy-start.1 = (bf16[64,8192]{1,0:T(8,128)(2,1)S(1)}, bf16[64,8192]{1,0:T(8,128)(2,1)}, u32[]{:S(2)}) copy-start(bf16[64,8192]{1,0:T(8,128)(2,1)} %param.24) | copy-start | bytes 3145732
  5.0 1.3 %collective-permute-start = (f32[8]{0:T(128)S(1)}, f32[8]{0:T(128)S(1)}, u32[]{:S(2)}, u32[]{:S(2)}) collective-permute-start(f32[8]{0:T(128)S(1)} %get-tuple-element.5), channel_id=1, source_target_pairs={{0,1},{1,0},{2,3},{3,2},{4,5},{5,4},{6,7},{7,6},{8,9},{9,8},{10,11... | collective-permute-start | bytes 104 | tf_op jit(solution)/shard_map/ppermute | solution.py:40
  6.4 1.3 %collective-permute-start.1 = (bf16[8,4096]{1,0:T(8,128)(2,1)S(1)}, bf16[8,4096]{1,0:T(8,128)(2,1)S(1)}, u32[]{:S(2)}, u32[]{:S(2)}) collective-permute-start(bf16[8,4096]{1,0:T(8,128)(2,1)S(1)} %fusion.5), channel_id=1, source_target_pairs={{0,1},{1,0},{2,3},{3,2},{4,5},{5,4},{6,7},{7,6},{8,9},{9,8},{10,11... | collective-permute-start | bytes 196616 | tf_op jit(solution)/shard_map/ppermute | solution.py:40
  8.8 16.4 %all-to-all-start = ((bf16[8,2,8192]{2,1,0:T(2,128)(2,1)}), bf16[8,2,8192]{2,1,0:T(2,128)(2,1)S(1)}, u32[]{:S(2)}, u32[]{:S(2)}) async-start(bf16[8,2,8192]{2,1,0:T(2,128)(2,1)} %all_to_all.8), calls=%async_computation | async-start | bytes 524288 | tf_op jit(solution)/shard_map/all_to_all | solution.py:143
  16.4 9.0 %copy-start.3 = (bf16[32,8192]{1,0:T(8,128)(2,1)S(1)}, bf16[32,8192]{1,0:T(8,128)(2,1)}, u32[]{:S(2)}) copy-start(bf16[32,8192]{1,0:T(8,128)(2,1)} %param.26) | copy-start | bytes 1572868
  25.6 2.0 %copy-start.2 = (bf16[64,8192]{1,0:T(8,128)(2,1)S(1)}, bf16[64,8192]{1,0:T(8,128)(2,1)}, u32[]{:S(2)}) copy-start(bf16[64,8192]{1,0:T(8,128)(2,1)} %param.23) | copy-start | bytes 3145732
  27.5 1.7 %collective-permute-start.3 = (f32[16,4096]{1,0:T(8,128)S(1)}, f32[16,4096]{1,0:T(8,128)}, u32[]{:S(2)}, u32[]{:S(2)}) collective-permute-start(f32[16,4096]{1,0:T(8,128)S(1)} %constant_dynamic-slice_fusion), channel_id=1, source_target_pairs={{0,1},{1,0},{2,3},{3,2},{4,5},{5,4},{6,7},{7,6},{8,9},{9,8},{10,11... | collective-permute-start | bytes 786440 | tf_op jit(solution)/shard_map/ppermute | solution.py:40
  30.4 4.8 %collective-permute-start.4 = (f32[2,4096]{1,0:T(2,128)S(1)}, f32[2,4096]{1,0:T(2,128)S(1)}, u32[]{:S(2)}, u32[]{:S(2)}) collective-permute-start(f32[2,4096]{1,0:T(2,128)S(1)} %get-tuple-element.13), channel_id=1, source_target_pairs={{0,2},{2,0},{4,6},{6,4},{8,10},{10,8},{12,14},{14,12},{1,3},{3,1},... | collective-permute-start | bytes 98312 | tf_op jit(solution)/shard_map/ppermute | solution.py:28
  31.9 15.3 %collective-permute-start.2 = (f32[8,4096]{1,0:T(8,128)S(1)}, f32[8,4096]{1,0:T(8,128)S(1)}, u32[]{:S(2)}, u32[]{:S(2)}) collective-permute-start(f32[8,4096]{1,0:T(8,128)S(1)} %constant_dynamic-slice_fusion.1), channel_id=1, source_target_pairs={{0,1},{1,0},{2,3},{3,2},{4,5},{5,4},{6,7},{7,6},{8,9},{9,8},{10,11... | collective-permute-start | bytes 393224 | tf_op jit(solution)/shard_map/ppermute | solution.py:40
  32.0 5.9 %collective-permute-start.5 = (f32[2,4096]{1,0:T(2,128)S(1)}, f32[2,4096]{1,0:T(2,128)S(1)}, u32[]{:S(2)}, u32[]{:S(2)}) collective-permute-start(f32[2,4096]{1,0:T(2,128)S(1)} %get-tuple-element.12), channel_id=1, source_target_pairs={{0,4},{2,6},{4,0},{6,2},{8,12},{10,14},{12,8},{14,10},{1,5},{3,7},... | collective-permute-start | bytes 98312 | tf_op jit(solution)/shard_map/ppermute | solution.py:28
  32.1 7.3 %collective-permute-start.6 = (f32[2,4096]{1,0:T(2,128)S(1)}, f32[2,4096]{1,0:T(2,128)S(1)}, u32[]{:S(2)}, u32[]{:S(2)}) collective-permute-start(f32[2,4096]{1,0:T(2,128)S(1)} %get-tuple-element.11), channel_id=1, source_target_pairs={{0,6},{2,4},{4,2},{6,0},{8,14},{10,12},{12,10},{14,8},{1,7},{3,5},... | collective-permute-start | bytes 98312 | tf_op jit(solution)/shard_map/ppermute | solution.py:28
  34.1 7.8 %collective-permute-start.7 = (f32[2,4096]{1,0:T(2,128)S(1)}, f32[2,4096]{1,0:T(2,128)S(1)}, u32[]{:S(2)}, u32[]{:S(2)}) collective-permute-start(f32[2,4096]{1,0:T(2,128)S(1)} %get-tuple-element.10), channel_id=1, source_target_pairs={{0,8},{2,10},{4,12},{6,14},{8,0},{10,2},{12,4},{14,6},{1,9},{3,11}... | collective-permute-start | bytes 98312 | tf_op jit(solution)/shard_map/ppermute | solution.py:28
  35.2 6.8 %collective-permute-start.8 = (f32[2,4096]{1,0:T(2,128)S(1)}, f32[2,4096]{1,0:T(2,128)S(1)}, u32[]{:S(2)}, u32[]{:S(2)}) collective-permute-start(f32[2,4096]{1,0:T(2,128)S(1)} %get-tuple-element.9), channel_id=1, source_target_pairs={{0,10},{2,8},{4,14},{6,12},{8,2},{10,0},{12,6},{14,4},{1,11},{3,9}... | collective-permute-start | bytes 98312 | tf_op jit(solution)/shard_map/ppermute | solution.py:28
  37.9 5.8 %collective-permute-start.9 = (f32[2,4096]{1,0:T(2,128)S(1)}, f32[2,4096]{1,0:T(2,128)S(1)}, u32[]{:S(2)}, u32[]{:S(2)}) collective-permute-start(f32[2,4096]{1,0:T(2,128)S(1)} %get-tuple-element.8), channel_id=1, source_target_pairs={{0,12},{2,14},{4,8},{6,10},{8,4},{10,6},{12,0},{14,2},{1,13},{3,15... | collective-permute-start | bytes 98312 | tf_op jit(solution)/shard_map/ppermute | solution.py:28
  39.5 6.7 %collective-permute-start.10 = (f32[2,4096]{1,0:T(2,128)S(1)}, f32[2,4096]{1,0:T(2,128)S(1)}, u32[]{:S(2)}, u32[]{:S(2)}) collective-permute-start(f32[2,4096]{1,0:T(2,128)S(1)} %get-tuple-element.7), channel_id=1, source_target_pairs={{0,14},{2,12},{4,10},{6,8},{8,6},{10,4},{12,2},{14,0},{1,15},{3,13... | collective-permute-start | bytes 98312 | tf_op jit(solution)/shard_map/ppermute | solution.py:28
